TPU v7x, 512 devices: a whole 4x4x16 slice. The times are simulated.
512 devices in a mesh: ref: 16 (over y_hi, x, core), dom: 32 (over y_lo, z).
Axes of the slice: x: 4, y: 4 (y_hi: 2, y_lo: 2; y = y_hi * 2 + y_lo), z: 16, core: 2. Of those that a mesh axis runs over, the one named last changes fastest.
Arguments:
- particles: bfloat16 [16384, 4096], P(('ref', 'dom'))
- inv_noise: float32 [16384], P(('ref', 'dom')), may hold values from 1 to 6
- candidates: int32 [16384, 8], P(('ref', 'dom')), may hold values from 0 to 127, as said below
- offsets: int32 [9, 2], replicated, may hold values from -2 to 2, as said below
- references: bfloat16 [128, 4096], P('ref')
Outputs:
- refreshed: bfloat16 [128, 4096], P('ref', 'dom')
- log_evidence: float32 [16384], P(('ref', 'dom'))
Inputs may be any that keep to these rules, and one draw needn't show every extreme that they name: `candidates`: each row names 8 different classes; class loads are uneven. `offsets`: 9 different shifts.
All inputs are finite; a program needn't handle non-finite values.
Results may differ from a plain program's by a relative error of at most 0.0038.
Values may be sent and summed in bfloat16 or wider, within the bound.
No kernel may reach another device: no remote copies, remote signals or barrier semaphores. Data moves between devices by JAX's collectives and lax.ppermute only.
A program may use at most 64 MiB of HBM per device.

v0:
```python
import jax
import jax.numpy as jnp
from jax import lax
from jax.sharding import PartitionSpec as P

SIDE = 64


def flat_roll(images, row_move, col_move):
    pixels = SIDE * SIDE
    moved = jnp.roll(images, row_move * SIDE, axis=1)
    col_mod = jnp.mod(col_move, SIDE)
    column = jnp.arange(pixels, dtype=jnp.int32) % SIDE
    inside = jnp.roll(moved, col_mod, axis=1)
    wrapped = jnp.roll(moved, col_mod - SIDE, axis=1)
    return jnp.where((column >= col_mod)[None, :], inside, wrapped)


def roll_set(images, offsets, sign):
    translated_image = []
    for shift_idx in range(offsets.shape[0]):
        translated_image.append(
            flat_roll(images, sign * offsets[shift_idx, 0], sign * offsets[shift_idx, 1])
        )
    return jnp.stack(translated_image, axis=1)


def per_device(particles, inv_noise, candidates, offsets, references):
    tile_size = references.shape[0]
    all_classes = tile_size * lax.axis_size("ref")
    stacked = roll_set(particles, offsets, -1)
    tile_rows = lax.all_gather(references, "ref", axis=0, tiled=True)
    tile_float = tile_rows.astype(jnp.float32)
    norms = jnp.sum(tile_float * tile_float, axis=1)
    translated_image = roll_set(tile_rows, offsets, 1)
    match_score = jnp.einsum(
        "vi,jti->vtj", particles, translated_image, preferred_element_type=jnp.float32
    )
    update = match_score - 0.5 * norms[None, None, :]
    score = inv_noise[:, None, None] * update
    classes = jnp.arange(all_classes, dtype=jnp.int32)
    permitted_mask = jnp.any(candidates[:, :, None] == classes[None, None, :], axis=1)
    masked = jnp.where(permitted_mask[:, None, :], score, -1e30)
    peak_val = jnp.max(masked, axis=(1, 2))
    denom_sum = jnp.sum(jnp.exp(masked - peak_val[:, None, None]), axis=(1, 2))
    evidence = peak_val + jnp.log(denom_sum)
    weight = jnp.where(
        permitted_mask[:, None, :], jnp.exp(masked - evidence[:, None, None]), 0.0
    ).astype(jnp.bfloat16)
    summed = lax.psum_scatter(
        jnp.einsum("psk,psq->kq", weight, stacked, preferred_element_type=jnp.float32),
        "ref",
        scatter_dimension=0,
        tiled=True,
    )
    shares = lax.psum_scatter(summed, "dom", scatter_dimension=1, tiled=True)
    row_power = lax.psum(jnp.sum(shares * shares, axis=1), "dom")
    refreshed = (shares / jnp.sqrt(row_power[:, None] / (SIDE * SIDE) + 1e-06)).astype(jnp.bfloat16)
    return (refreshed, evidence)


def solution(mesh):
    in_specs = (
        P(("ref", "dom"), None),
        P(("ref", "dom")),
        P(("ref", "dom"), None),
        P(),
        P("ref", None),
    )
    out_specs = (P("ref", "dom"), P(("ref", "dom")))
    return jax.shard_map(
        per_device, mesh=mesh, in_specs=in_specs, out_specs=out_specs, check_vma=False
    )
```

profile of v0, /device:TPU:6, one launch (start us, length us, event | category | flops | bytes accessed | tf_op | source)
XLA Modules:
  0.0 408.3 jit_solution(2184901198757844488)
XLA Ops:
  7.2 0.7 all-gather.2.cloned.1.call-update
  7.9 2.1 fusion.120
  39.1 1.0 constant_dynamic-update-slice_fusion.3
  40.1 1.0 constant_dynamic-update-slice_fusion.2
  41.5 1.0 constant_dynamic-slice_fusion.5
  42.5 0.6 fusion.91
  43.1 0.6 fusion.86
  43.7 0.6 fusion.81
  44.3 0.6 fusion.76
  44.9 0.6 fusion.71
  45.5 0.6 fusion.66
  46.1 0.6 fusion.61
  54.6 21.1 %all-gather.2.cloned.1.call-done = bf16[128,4096]{1,0:T(8,128)(2,1)} async-done(((bf16[8,4096]{1,0:T(8,128)(2,1)}), bf16[128,4096]{1,0:T(8,128)(2,1)}) %all-gather.2.cloned.1.call-update) | async-done | bytes 1048592 | tf_op jit(solution)/shard_map/all_gather | solution.py:32
  75.7 1.6 multiply_reduce_fusion
  77.3 1.3 constant_dynamic-update-slice_fusion.1
  78.7 5.6 %constant_dynamic-slice_fusion.9 = (bf16[128,4096]{1,0:T(8,128)(2,1)S(1)}, bf16[128,4096]{1,0:T(8,128)(2,1)S(1)}, bf16[128,4096]{1,0:T(8,128)(2,1)S(1)}, bf16[12...) fusion(bf16[128,8192]{1,0:T(8,128)(2,1)S(1)} %constant_dynamic-, ...), kind=kLoop, calls=%fused_computation.190 | loop fusion | bytes 18874404 | tf_op jit(solution)/shard_map/jit(_roll_dynamic)/dynamic_slice | solution.py:11
  84.3 1.7 fusion.46
  86.0 1.8 fusion.41
  87.8 1.8 fusion.36
  89.6 1.8 fusion.31
  91.3 1.8 fusion.26
  93.1 2.0 fusion.21
  95.1 1.8 fusion.16
  97.0 1.8 fusion.11
  98.7 1.8 fusion.6
  100.6 3.0 fusion.121
  103.8 2.2 convolution_bitcast_fusion
  106.0 93.1 %reduce-scatter.3.cloned.1.call-done = f32[8,4096]{1,0:T(8,128)} async-done(((f32[128,4096]{1,0:T(8,128)}), f32[8,4096]{1,0:T(8,128)}) %reduce-scatter.3.cloned.1.call-update) | async-done | bytes 131088 | tf_op jit(solution)/shard_map/reduce_scatter | solution.py:50
  199.2 139.1 %reduce-scatter.5.cloned.1.call-done = f32[8,128]{1,0:T(8,128)} async-done(((f32[8,4096]{1,0:T(8,128)}), f32[8,128]{1,0:T(8,128)}) %reduce-scatter.5.cloned.1.call-update) | async-done | bytes 4112 | tf_op jit(solution)/shard_map/reduce_scatter | solution.py:56
  338.3 0.8 multiply_reduce_fusion.1
  339.1 61.3 %psum.7 = f32[8]{0:T(128)S(1)} all-reduce(f32[8]{0:T(128)S(1)} %multiply_reduce_fusion.1), channel_id=1, replica_groups=mesh['ref'=16,'dom'=32] {'dom'}, use_global_device_ids=true, to_apply=%region_7.10 | all-reduce | flops 8 | bytes 64 | tf_op jit(solution)/shard_map/psum | solution.py:57
  400.4 1.3 divide_convert_fusion
  (34 shorter events, 2.0 us)
Async XLA Ops:
  7.2 68.5 %all-gather.2.cloned.1.call-start = ((), (), s32[]{:S(2)}) async-start(), calls=%async_computation.2 | async-start | bytes 1114112 | tf_op jit(solution)/shard_map/all_gather | solution.py:32
  7.9 191.3 %reduce-scatter.3.cloned.1.call-start = ((), (), s32[]{:S(2)}) async-start(), calls=%async_computation.3 | async-start | bytes 2228224 | tf_op jit(solution)/shard_map/reduce_scatter | solution.py:50
  43.1 10.0 %copy-start.2 = (s32[32,8]{0,1:T(8,128)S(1)}, s32[32,8]{0,1:T(8,128)}, u32[]{:S(2)}) copy-start(s32[32,8]{0,1:T(8,128)} %param.11) | copy-start | bytes 3076
  75.7 2.9 copy-start
  96.9 3.6 copy-start.1
  96.9 3.6 copy-start.3
  103.8 2.2 copy-start.4
  106.0 232.3 %reduce-scatter.5.cloned.1.call-start = ((), (), s32[]{:S(2)}) async-start(), calls=%async_computation.4 | async-start | bytes 135168 | tf_op jit(solution)/shard_map/reduce_scatter | solution.py:56
Sparse Core Ops, SparseCore 0:
  11.3 64.3 all-gather.1
  106.1 93.0 reduce-scatter.2
  201.9 136.3 reduce-scatter.4
where the time goes:
time: 409 us; the launch traced here: 408 us
  waiting for transfers between devices  254 us (62%)
  blocking collectives  61.3 us (15%)
  between operations  49.9 us (12%)
  other arithmetic  25.7 us (6%)
  local copies, waits for them, and re-layouts  12.1 us (3%)
  matrix products  5.16 us (1%)
    reduce_scatter x1, waiting for transfers between devices, per_device(): shares = lax.psum_scatter(summed, 'dom', scatter_dimension=1, tiled=True)  139 us
    reduce_scatter x1, waiting for transfers between devices, per_device(): lax.psum_scatter(jnp.einsum('psk,psq->kq', weight, stacked, preferred_ele...  93.1 us
    psum x1, blocking collectives, per_device(): row_power = lax.psum(jnp.sum(shares * shares, axis=1), 'dom')  61.3 us
    all_gather x1, waiting for transfers between devices, per_device(): tile_rows = lax.all_gather(references, 'ref', axis=0, tiled=True)  21.1 us
    unnamed x16, other arithmetic  19.2 us
  transfers between devices with their start and end apart: 3, of which 3 were waited for; matrix products, arithmetic and copies ran while one was open for 3% of the time, Pallas kernels for 0%

commit v1 on v0

--- a/solution.py
+++ b/solution.py
@@ -1,9 +1,25 @@
 import jax
 import jax.numpy as jnp
 from jax import lax
+from jax.sharding import Mesh
 from jax.sharding import PartitionSpec as P
 
 SIDE = 64
+REF = ("yh", "x", "c")
+DOM = ("yl", "z")
+ALL = REF + DOM
+HALVING = (
+    ("c", 2, 1),
+    ("yl", 2, 1),
+    ("x", 4, 1),
+    ("z", 16, 1),
+    ("yh", 2, 1),
+    ("x", 4, 2),
+    ("z", 16, 2),
+    ("z", 16, 4),
+    ("z", 16, 8),
+)
+DOUBLING = (("yl", 2, 1), ("z", 16, 1), ("z", 16, 2), ("z", 16, 4), ("z", 16, 8))
 
 
 def flat_roll(images, row_move, col_move):
@@ -25,11 +41,26 @@
     return jnp.stack(translated_image, axis=1)
 
 
+def partner(axis, size, bit):
+    return [(i, i ^ bit) for i in range(size)]
+
+
+def reduce_blocks(partial):
+    t = partial.reshape(2, 2, 2, 2, 8, 2, 2, 2, 2, 2, 128)
+    t = t.transpose(3, 5, 2, 9, 0, 1, 8, 7, 6, 4, 10)
+    for axis, size, bit in HALVING:
+        mine = (lax.axis_index(axis) // bit) % 2
+        keep = lax.dynamic_index_in_dim(t, mine, 0, keepdims=False)
+        send = lax.dynamic_index_in_dim(t, 1 - mine, 0, keepdims=False)
+        t = keep + lax.ppermute(send, axis, partner(axis, size, bit))
+    return t
+
+
 def per_device(particles, inv_noise, candidates, offsets, references):
     tile_size = references.shape[0]
-    all_classes = tile_size * lax.axis_size("ref")
+    all_classes = tile_size * 16
     stacked = roll_set(particles, offsets, -1)
-    tile_rows = lax.all_gather(references, "ref", axis=0, tiled=True)
+    tile_rows = lax.all_gather(references, REF, axis=0, tiled=True)
     tile_float = tile_rows.astype(jnp.float32)
     norms = jnp.sum(tile_float * tile_float, axis=1)
     translated_image = roll_set(tile_rows, offsets, 1)
@@ -47,27 +78,26 @@
     weight = jnp.where(
         permitted_mask[:, None, :], jnp.exp(masked - evidence[:, None, None]), 0.0
     ).astype(jnp.bfloat16)
-    summed = lax.psum_scatter(
-        jnp.einsum("psk,psq->kq", weight, stacked, preferred_element_type=jnp.float32),
-        "ref",
-        scatter_dimension=0,
-        tiled=True,
-    )
-    shares = lax.psum_scatter(summed, "dom", scatter_dimension=1, tiled=True)
-    row_power = lax.psum(jnp.sum(shares * shares, axis=1), "dom")
+    partial = jnp.einsum("psk,psq->kq", weight, stacked, preferred_element_type=jnp.float32)
+    shares = reduce_blocks(partial)
+    row_power = jnp.sum(shares * shares, axis=1)
+    for axis, size, bit in DOUBLING:
+        row_power = row_power + lax.ppermute(row_power, axis, partner(axis, size, bit))
     refreshed = (shares / jnp.sqrt(row_power[:, None] / (SIDE * SIDE) + 1e-06)).astype(jnp.bfloat16)
     return (refreshed, evidence)
 
 
 def solution(mesh):
+    assert mesh.devices.shape == (16, 32)
+    fine = Mesh(mesh.devices.reshape(2, 4, 2, 2, 16), ALL)
     in_specs = (
-        P(("ref", "dom"), None),
-        P(("ref", "dom")),
-        P(("ref", "dom"), None),
+        P(ALL, None),
+        P(ALL),
+        P(ALL, None),
         P(),
-        P("ref", None),
+        P(REF, None),
     )
-    out_specs = (P("ref", "dom"), P(("ref", "dom")))
+    out_specs = (P(REF, DOM), P(ALL))
     return jax.shard_map(
-        per_device, mesh=mesh, in_specs=in_specs, out_specs=out_specs, check_vma=False
+        per_device, mesh=fine, in_specs=in_specs, out_specs=out_specs, check_vma=False
     )

time: 409 us -> 239 us (0.58)
  waiting for transfers between devices: 254 us -> 73.1 us
  starting transfers between devices: 0.12 us -> 71.3 us
  blocking collectives: 61.3 us -> 0 us
    reduce_scatter x2 -> x0, waiting for transfers between devices: 232 us -> none  [the longest x1 139 us: per_device(): shares = lax.psum_scatter(summed, 'dom', scatter_dimension=1, tiled=True)]
    ppermute x0 -> x14, starting transfers between devices: none -> 71.3 us  [the longest x9 41.3 us: reduce_blocks(): t = keep + lax.ppermute(send, axis, partner(axis, size, bit))]
    psum x1 -> x0, blocking collectives: 61.3 us -> none  [per_device(): row_power = lax.psum(jnp.sum(shares * shares, axis=1), 'dom')]
    ppermute x0 -> x14, waiting for transfers between devices: none -> 51.5 us  [the longest x9 40.7 us: reduce_blocks(): t = keep + lax.ppermute(send, axis, partner(axis, size, bit))]
  transfers between devices with their start and end apart: 3 -> 15, of which waited for: 3 -> 15; matrix products, arithmetic and copies ran while one was open for 3% -> 4% of each run, Pallas kernels for 0% -> 0%
where the time goes in v1:
time: 239 us; the launch traced here: 237 us
  waiting for transfers between devices  73.1 us (31%)
  starting transfers between devices  71.3 us (30%)
  between operations  50.8 us (21%)
  other arithmetic  26 us (11%)
  local copies, waits for them, and re-layouts  12.4 us (5%)
  matrix products  3.82 us (2%)
    ppermute x9, starting transfers between devices, reduce_blocks(): t = keep + lax.ppermute(send, axis, partner(axis, size, bit))  41.3 us
    ppermute x9, waiting for transfers between devices, reduce_blocks(): t = keep + lax.ppermute(send, axis, partner(axis, size, bit))  40.7 us
    ppermute x5, starting transfers between devices, per_device(): lax.ppermute(row_power, axis, partner(axis, size, bit))  29.9 us
    all_gather x1, waiting for transfers between devices, per_device(): tile_rows = lax.all_gather(references, REF, axis=0, tiled=True)  21 us
    unnamed x16, other arithmetic  19.2 us
    ppermute x5, waiting for transfers between devices, per_device(): lax.ppermute(row_power, axis, partner(axis, size, bit))  10.8 us
    dynamic_slice x2, local copies, waits for them, and re-layouts, flat_roll(): moved = jnp.roll(images, row_move * SIDE, axis=1)  6.6 us
  transfers between devices with their start and end apart: 15, of which 15 were waited for; matrix products, arithmetic and copies ran while one was open for 4% of the time, Pallas kernels for 0%

profile of v1, /device:TPU:6, one launch (start us, length us, event | category | flops | bytes accessed | tf_op | source)
XLA Modules:
  0.0 237.4 jit_solution(4599199633924402682)
XLA Ops:
  7.9 2.0 fusion.130
  54.7 21.0 %all-gather.2.cloned.1.call-done = bf16[128,4096]{1,0:T(8,128)(2,1)} async-done(((bf16[8,4096]{1,0:T(8,128)(2,1)}), bf16[128,4096]{1,0:T(8,128)(2,1)}) %all-gather.2.cloned.1.call-update) | async-done | bytes 1048592 | tf_op jit(solution)/shard_map/all_gather | solution.py:63
  78.7 5.6 %constant_dynamic-slice_fusion.9 = (bf16[128,4096]{1,0:T(8,128)(2,1)S(1)}, bf16[128,4096]{1,0:T(8,128)(2,1)S(1)}, bf16[128,4096]{1,0:T(8,128)(2,1)S(1)}, bf16[12...) fusion(bf16[128,8192]{1,0:T(8,128)(2,1)S(1)} %constant_dynamic-, ...), kind=kLoop, calls=%fused_computation.201 | loop fusion | bytes 18874404 | tf_op jit(solution)/shard_map/jit(_roll_dynamic)/dynamic_slice | solution.py:27
  91.4 1.8 fusion.26
  93.2 2.0 fusion.21
  95.2 1.8 fusion.16
  100.6 3.0 %fusion.131 = (f32[32]{0:T(128)S(1)}, f32[32,9,128]{2,0,1:T(8,128)S(1)}) fusion(f32[128]{0:T(128)S(1)} %broadcast_multiply_fusion, bf16[128,9,4096]{2,0,1:T(8,128)(2,1)S(1)} %fusion.6, bf16[32,4096]{1,0:T(8,128)(2,1)S(1)} %copy-done.3, f32[32]{0:T(128)S(1)} %copy-done.5, pred[32,128]{1,0:T(8,128)(4,1)S(1)} %fusion.94), kind=kOutput, calls=%fused_computation.257 | convolution fusion | flops 302137312 | bytes 9851648 | tf_op jit(solution)/shard_map/vi,jti->vtj/dot_general | solution.py:67
  104.8 2.1 collective-permute-start
  107.0 2.5 %collective-permute-done = f32[2,2,2,2,2,2,2,2,8,128]{9,8,2,5,6,7,0,1,4,3:T(8,128)} collective-permute-done((f32[2,2,2,2,2,2,2,2,8,128]{9,8,2,5,6,7,0,1,4,3:T(8,128)S(1)}, f32[2,2,2,2,2,2,2,2,8,128]{9,8,2,5,6,7,0,1,4,3:T(8,128)}, u32[]{:S(2)}, u32[]{:S(2)}) %collective-permute-start) | collective-permute-done | bytes 1048608 | tf_op jit(solution)/shard_map/ppermute | solution.py:55
  111.0 2.5 %collective-permute-start.1 = (f32[2,2,2,2,2,2,2,8,128]{8,7,1,4,5,6,0,3,2:T(8,128)S(1)}, f32[2,2,2,2,2,2,2,8,128]{8,7,1,4,5,6,0,3,2:T(8,128)S(1)}, u32[]{:S(2)}, u32[]{:S(2)}) collective-permute-start(f32[2,2,2,2,2,2,2,8,128]{8,7,1,4,5,6,0,3,2:T(8,128)S(1)} %dynamic-slice_bitcast_fusion.1), channel_id=1, source_target_pairs={{0,16},{16,0},{1,17},{17,1},{2,18},{18,2},{3,19},{19,3},{4,20},{20... | collective-permute-start | bytes 1572872 | tf_op jit(solution)/shard_map/ppermute | solution.py:55
  113.5 13.4 %collective-permute-done.1 = f32[2,2,2,2,2,2,2,8,128]{8,7,1,4,5,6,0,3,2:T(8,128)S(1)} collective-permute-done((f32[2,2,2,2,2,2,2,8,128]{8,7,1,4,5,6,0,3,2:T(8,128)S(1)}, f32[2,2,2,2,2,2,2,8,128]{8,7,1,4,5,6,0,3,2:T(8,128)S(1)}, u32[]{:S(2)}, u32[]{:S(2)}) %collective-permute-start.1) | collective-permute-done | bytes 524320 | tf_op jit(solution)/shard_map/ppermute | solution.py:55
  127.1 1.9 collective-permute-start.2
  129.0 7.5 %collective-permute-done.2 = f32[2,2,2,2,2,2,8,128]{7,6,5,4,3,2,1,0:T(8,128)S(1)} collective-permute-done((f32[2,2,2,2,2,2,8,128]{7,6,5,4,3,2,1,0:T(8,128)S(1)}, f32[2,2,2,2,2,2,8,128]{7,6,5,4,3,2,1,0:T(8,128)S(1)}, u32[]{:S(2)}, u32[]{:S(2)}) %collective-permute-start.2) | collective-permute-done | bytes 262176 | tf_op jit(solution)/shard_map/ppermute | solution.py:55
  136.6 3.5 %collective-permute-start.3 = (f32[2,2,2,2,2,8,128]{6,5,4,3,2,1,0:T(8,128)S(1)}, f32[2,2,2,2,2,8,128]{6,5,4,3,2,1,0:T(8,128)S(1)}, u32[]{:S(2)}, u32[]{:S(2)}) collective-permute-start(f32[2,2,2,2,2,8,128]{6,5,4,3,2,1,0:T(8,128)S(1)} %dynamic-slice_bitcast_fusion.2), channel_id=1, source_target_pairs={{0,1},{1,0},{2,3},{3,2},{4,5},{5,4},{6,7},{7,6},{8,9},{9,8},{10,11... | collective-permute-start | bytes 393224 | tf_op jit(solution)/shard_map/ppermute | solution.py:55
  140.1 3.4 %collective-permute-done.3 = f32[2,2,2,2,2,8,128]{6,5,4,3,2,1,0:T(8,128)S(1)} collective-permute-done((f32[2,2,2,2,2,8,128]{6,5,4,3,2,1,0:T(8,128)S(1)}, f32[2,2,2,2,2,8,128]{6,5,4,3,2,1,0:T(8,128)S(1)}, u32[]{:S(2)}, u32[]{:S(2)}) %collective-permute-start.3) | collective-permute-done | bytes 131104 | tf_op jit(solution)/shard_map/ppermute | solution.py:55
  143.5 3.1 %collective-permute-start.4 = (f32[2,2,2,2,8,128]{5,4,3,2,1,0:T(8,128)S(1)}, f32[2,2,2,2,8,128]{5,4,3,2,1,0:T(8,128)S(1)}, u32[]{:S(2)}, u32[]{:S(2)}) collective-permute-start(f32[2,2,2,2,8,128]{5,4,3,2,1,0:T(8,128)S(1)} %dynamic-slice_bitcast_fusion.3), channel_id=1, source_target_pairs={{0,256},{256,0},{1,257},{257,1},{2,258},{258,2},{3,259},{259,3},{4... | collective-permute-start | bytes 196616 | tf_op jit(solution)/shard_map/ppermute | solution.py:55
  146.6 4.5 %collective-permute-done.4 = f32[2,2,2,2,8,128]{5,4,3,2,1,0:T(8,128)S(1)} collective-permute-done((f32[2,2,2,2,8,128]{5,4,3,2,1,0:T(8,128)S(1)}, f32[2,2,2,2,8,128]{5,4,3,2,1,0:T(8,128)S(1)}, u32[]{:S(2)}, u32[]{:S(2)}) %collective-permute-start.4) | collective-permute-done | bytes 65568 | tf_op jit(solution)/shard_map/ppermute | solution.py:55
  151.2 3.4 %collective-permute-start.5 = (f32[2,2,2,8,128]{4,3,2,1,0:T(8,128)S(1)}, f32[2,2,2,8,128]{4,3,2,1,0:T(8,128)S(1)}, u32[]{:S(2)}, u32[]{:S(2)}) collective-permute-start(f32[2,2,2,8,128]{4,3,2,1,0:T(8,128)S(1)} %dynamic-slice_bitcast_fusion.4), channel_id=1, source_target_pairs={{0,128},{64,192},{128,0},{192,64},{1,129},{65,193},{129,1},{193,65... | collective-permute-start | bytes 98312 | tf_op jit(solution)/shard_map/ppermute | solution.py:55
  154.6 3.9 %collective-permute-done.5 = f32[2,2,2,8,128]{4,3,2,1,0:T(8,128)S(1)} collective-permute-done((f32[2,2,2,8,128]{4,3,2,1,0:T(8,128)S(1)}, f32[2,2,2,8,128]{4,3,2,1,0:T(8,128)S(1)}, u32[]{:S(2)}, u32[]{:S(2)}) %collective-permute-start.5) | collective-permute-done | bytes 32800 | tf_op jit(solution)/shard_map/ppermute | solution.py:55
  158.6 4.4 %collective-permute-start.6 = (f32[2,2,8,128]{3,2,1,0:T(8,128)S(1)}, f32[2,2,8,128]{3,2,1,0:T(8,128)S(1)}, u32[]{:S(2)}, u32[]{:S(2)}) collective-permute-start(f32[2,2,8,128]{3,2,1,0:T(8,128)S(1)} %fusion.101), channel_id=1, source_target_pairs={{0,2},{1,3},{2,0},{3,1},{4,6},{5,7},{6,4},{7,5},{8,10},{9,11},{10,... | collective-permute-start | bytes 49160 | tf_op jit(solution)/shard_map/ppermute | solution.py:55
  163.0 2.0 collective-permute-done.6
  165.1 7.6 %collective-permute-start.7 = (f32[2,8,128]{2,1,0:T(8,128)S(1)}, f32[2,8,128]{2,1,0:T(8,128)S(1)}, u32[]{:S(2)}, u32[]{:S(2)}) collective-permute-start(f32[2,8,128]{2,1,0:T(8,128)S(1)} %fusion.125), channel_id=1, source_target_pairs={{0,4},{1,5},{2,6},{3,7},{4,0},{5,1},{6,2},{7,3},{8,12},{9,13},{10,... | collective-permute-start | bytes 24584 | tf_op jit(solution)/shard_map/ppermute | solution.py:55
  174.5 12.8 %collective-permute-start.8 = (f32[8,128]{1,0:T(8,128)S(1)}, f32[8,128]{1,0:T(8,128)S(1)}, u32[]{:S(2)}, u32[]{:S(2)}) collective-permute-start(f32[8,128]{1,0:T(8,128)S(1)} %fusion.128), channel_id=1, source_target_pairs={{0,8},{1,9},{2,10},{3,11},{4,12},{5,13},{6,14},{7,15},{8,0},{9,1},... | collective-permute-start | bytes 12296 | tf_op jit(solution)/shard_map/ppermute | solution.py:55
  189.1 2.5 %collective-permute-start.9 = (f32[8]{0:T(128)S(1)}, f32[8]{0:T(128)S(1)}, u32[]{:S(2)}, u32[]{:S(2)}) collective-permute-start(f32[8]{0:T(128)S(1)} %multiply_reduce_fusion.1), channel_id=1, source_target_pairs={{0,16},{16,0},{1,17},{17,1},{2,18},{18,2},{3,19},{19,3},{4,20},{20... | collective-permute-start | bytes 104 | tf_op jit(solution)/shard_map/ppermute | solution.py:85
  191.6 3.0 %collective-permute-done.9 = f32[8]{0:T(128)S(1)} collective-permute-done((f32[8]{0:T(128)S(1)}, f32[8]{0:T(128)S(1)}, u32[]{:S(2)}, u32[]{:S(2)}) %collective-permute-start.9) | collective-permute-done | bytes 64 | tf_op jit(solution)/shard_map/ppermute | solution.py:85
  194.6 3.2 %collective-permute-start.10 = (f32[8]{0:T(128)S(1)}, f32[8]{0:T(128)S(1)}, u32[]{:S(2)}, u32[]{:S(2)}) collective-permute-start(f32[8]{0:T(128)S(1)} %add.434), channel_id=1, source_target_pairs={{0,1},{1,0},{2,3},{3,2},{4,5},{5,4},{6,7},{7,6},{8,9},{9,8},{10,11... | collective-permute-start | bytes 104 | tf_op jit(solution)/shard_map/ppermute | solution.py:85
  197.8 2.2 collective-permute-done.10
  200.0 4.2 %collective-permute-start.11 = (f32[8]{0:T(128)S(1)}, f32[8]{0:T(128)S(1)}, u32[]{:S(2)}, u32[]{:S(2)}) collective-permute-start(f32[8]{0:T(128)S(1)} %add.435), channel_id=1, source_target_pairs={{0,2},{1,3},{2,0},{3,1},{4,6},{5,7},{6,4},{7,5},{8,10},{9,11},{10,... | collective-permute-start | bytes 104 | tf_op jit(solution)/shard_map/ppermute | solution.py:85
  204.2 2.1 collective-permute-done.11
  206.4 7.4 %collective-permute-start.12 = (f32[8]{0:T(128)S(1)}, f32[8]{0:T(128)S(1)}, u32[]{:S(2)}, u32[]{:S(2)}) collective-permute-start(f32[8]{0:T(128)S(1)} %add.436), channel_id=1, source_target_pairs={{0,4},{1,5},{2,6},{3,7},{4,0},{5,1},{6,2},{7,3},{8,12},{9,13},{10,... | collective-permute-start | bytes 104 | tf_op jit(solution)/shard_map/ppermute | solution.py:85
  213.8 1.9 collective-permute-done.12
  215.7 12.6 %collective-permute-start.13 = (f32[8]{0:T(128)S(1)}, f32[8]{0:T(128)S(1)}, u32[]{:S(2)}, u32[]{:S(2)}) collective-permute-start(f32[8]{0:T(128)S(1)} %add.437), channel_id=1, source_target_pairs={{0,8},{1,9},{2,10},{3,11},{4,12},{5,13},{6,14},{7,15},{8,0},{9,1},... | collective-permute-start | bytes 104 | tf_op jit(solution)/shard_map/ppermute | solution.py:85
  (81 shorter events, 31.6 us)
Async XLA Ops:
  7.2 68.5 %all-gather.2.cloned.1.call-start = ((), (), s32[]{:S(2)}) async-start(), calls=%async_computation | async-start | bytes 1114112 | tf_op jit(solution)/shard_map/all_gather | solution.py:63
  43.0 10.1 %copy-start.4 = (s32[32,8]{0,1:T(8,128)S(1)}, s32[32,8]{0,1:T(8,128)}, u32[]{:S(2)}) copy-start(s32[32,8]{0,1:T(8,128)} %param.11) | copy-start | bytes 3076
  54.7 24.0 %copy-start.1 = (bf16[32,9,4096]{2,0,1:T(8,128)(2,1)}, bf16[32,9,4096]{2,0,1:T(8,128)(2,1)S(1)}, u32[]{:S(2)}) copy-start(bf16[32,9,4096]{2,0,1:T(8,128)(2,1)S(1)} %fusion.51) | copy-start | bytes 7077892
  75.7 2.9 %copy-start = (bf16[128,4096]{1,0:T(8,128)(2,1)S(1)}, bf16[128,4096]{1,0:T(8,128)(2,1)}, u32[]{:S(2)}) copy-start(bf16[128,4096]{1,0:T(8,128)(2,1)} %all-gather.2.cloned.1.call-done) | copy-start | bytes 3145732
  97.0 3.6 %copy-start.3 = (bf16[32,4096]{1,0:T(8,128)(2,1)S(1)}, bf16[32,4096]{1,0:T(8,128)(2,1)}, u32[]{:S(2)}) copy-start(bf16[32,4096]{1,0:T(8,128)(2,1)} %param.9) | copy-start | bytes 786436
  97.0 3.6 %copy-start.5 = (f32[32]{0:T(128)S(1)}, f32[32]{0:T(128)}, u32[]{:S(2)}) copy-start(f32[32]{0:T(128)} %param.10) | copy-start | bytes 388
  100.6 3.2 %copy-start.2 = (bf16[32,9,4096]{2,0,1:T(8,128)(2,1)S(1)}, bf16[32,9,4096]{2,0,1:T(8,128)(2,1)}, u32[]{:S(2)}) copy-start(bf16[32,9,4096]{2,0,1:T(8,128)(2,1)} %copy-done.1) | copy-start | bytes 7077892
  103.8 0.8 copy-start.6
  104.8 4.7 %collective-permute-start = (f32[2,2,2,2,2,2,2,2,8,128]{9,8,2,5,6,7,0,1,4,3:T(8,128)S(1)}, f32[2,2,2,2,2,2,2,2,8,128]{9,8,2,5,6,7,0,1,4,3:T(8,128)}, u32[]{:S(2)}, u32[]{:S(2)}) collective-permute-start(f32[2,2,2,2,2,2,2,2,8,128]{9,8,2,5,6,7,0,1,4,3:T(8,128)S(1)} %dynamic-slice_bitcast_fusion), channel_id=1, source_target_pairs={{0,32},{32,0},{1,33},{33,1},{2,34},{34,2},{3,35},{35,3},{4,36},{36... | collective-permute-start | bytes 3145736 | tf_op jit(solution)/shard_map/ppermute | solution.py:55
  111.0 15.9 %collective-permute-start.1 = (f32[2,2,2,2,2,2,2,8,128]{8,7,1,4,5,6,0,3,2:T(8,128)S(1)}, f32[2,2,2,2,2,2,2,8,128]{8,7,1,4,5,6,0,3,2:T(8,128)S(1)}, u32[]{:S(2)}, u32[]{:S(2)}) collective-permute-start(f32[2,2,2,2,2,2,2,8,128]{8,7,1,4,5,6,0,3,2:T(8,128)S(1)} %dynamic-slice_bitcast_fusion.1), channel_id=1, source_target_pairs={{0,16},{16,0},{1,17},{17,1},{2,18},{18,2},{3,19},{19,3},{4,20},{20... | collective-permute-start | bytes 1572872 | tf_op jit(solution)/shard_map/ppermute | solution.py:55
  127.1 9.5 %collective-permute-start.2 = (f32[2,2,2,2,2,2,8,128]{7,6,5,4,3,2,1,0:T(8,128)S(1)}, f32[2,2,2,2,2,2,8,128]{7,6,5,4,3,2,1,0:T(8,128)S(1)}, u32[]{:S(2)}, u32[]{:S(2)}) collective-permute-start(f32[2,2,2,2,2,2,8,128]{7,6,5,4,3,2,1,0:T(8,128)S(1)} %bitcast.168), channel_id=1, source_target_pairs={{0,64},{64,0},{128,192},{192,128},{1,65},{65,1},{129,193},{193,129... | collective-permute-start | bytes 786440 | tf_op jit(solution)/shard_map/ppermute | solution.py:55
  136.6 6.9 %collective-permute-start.3 = (f32[2,2,2,2,2,8,128]{6,5,4,3,2,1,0:T(8,128)S(1)}, f32[2,2,2,2,2,8,128]{6,5,4,3,2,1,0:T(8,128)S(1)}, u32[]{:S(2)}, u32[]{:S(2)}) collective-permute-start(f32[2,2,2,2,2,8,128]{6,5,4,3,2,1,0:T(8,128)S(1)} %dynamic-slice_bitcast_fusion.2), channel_id=1, source_target_pairs={{0,1},{1,0},{2,3},{3,2},{4,5},{5,4},{6,7},{7,6},{8,9},{9,8},{10,11... | collective-permute-start | bytes 393224 | tf_op jit(solution)/shard_map/ppermute | solution.py:55
  143.5 7.7 %collective-permute-start.4 = (f32[2,2,2,2,8,128]{5,4,3,2,1,0:T(8,128)S(1)}, f32[2,2,2,2,8,128]{5,4,3,2,1,0:T(8,128)S(1)}, u32[]{:S(2)}, u32[]{:S(2)}) collective-permute-start(f32[2,2,2,2,8,128]{5,4,3,2,1,0:T(8,128)S(1)} %dynamic-slice_bitcast_fusion.3), channel_id=1, source_target_pairs={{0,256},{256,0},{1,257},{257,1},{2,258},{258,2},{3,259},{259,3},{4... | collective-permute-start | bytes 196616 | tf_op jit(solution)/shard_map/ppermute | solution.py:55
  151.2 7.3 %collective-permute-start.5 = (f32[2,2,2,8,128]{4,3,2,1,0:T(8,128)S(1)}, f32[2,2,2,8,128]{4,3,2,1,0:T(8,128)S(1)}, u32[]{:S(2)}, u32[]{:S(2)}) collective-permute-start(f32[2,2,2,8,128]{4,3,2,1,0:T(8,128)S(1)} %dynamic-slice_bitcast_fusion.4), channel_id=1, source_target_pairs={{0,128},{64,192},{128,0},{192,64},{1,129},{65,193},{129,1},{193,65... | collective-permute-start | bytes 98312 | tf_op jit(solution)/shard_map/ppermute | solution.py:55
  158.6 6.5 %collective-permute-start.6 = (f32[2,2,8,128]{3,2,1,0:T(8,128)S(1)}, f32[2,2,8,128]{3,2,1,0:T(8,128)S(1)}, u32[]{:S(2)}, u32[]{:S(2)}) collective-permute-start(f32[2,2,8,128]{3,2,1,0:T(8,128)S(1)} %fusion.101), channel_id=1, source_target_pairs={{0,2},{1,3},{2,0},{3,1},{4,6},{5,7},{6,4},{7,5},{8,10},{9,11},{10,... | collective-permute-start | bytes 49160 | tf_op jit(solution)/shard_map/ppermute | solution.py:55
  165.1 9.4 %collective-permute-start.7 = (f32[2,8,128]{2,1,0:T(8,128)S(1)}, f32[2,8,128]{2,1,0:T(8,128)S(1)}, u32[]{:S(2)}, u32[]{:S(2)}) collective-permute-start(f32[2,8,128]{2,1,0:T(8,128)S(1)} %fusion.125), channel_id=1, source_target_pairs={{0,4},{1,5},{2,6},{3,7},{4,0},{5,1},{6,2},{7,3},{8,12},{9,13},{10,... | collective-permute-start | bytes 24584 | tf_op jit(solution)/shard_map/ppermute | solution.py:55
  174.5 14.4 %collective-permute-start.8 = (f32[8,128]{1,0:T(8,128)S(1)}, f32[8,128]{1,0:T(8,128)S(1)}, u32[]{:S(2)}, u32[]{:S(2)}) collective-permute-start(f32[8,128]{1,0:T(8,128)S(1)} %fusion.128), channel_id=1, source_target_pairs={{0,8},{1,9},{2,10},{3,11},{4,12},{5,13},{6,14},{7,15},{8,0},{9,1},... | collective-permute-start | bytes 12296 | tf_op jit(solution)/shard_map/ppermute | solution.py:55
  189.1 5.5 %collective-permute-start.9 = (f32[8]{0:T(128)S(1)}, f32[8]{0:T(128)S(1)}, u32[]{:S(2)}, u32[]{:S(2)}) collective-permute-start(f32[8]{0:T(128)S(1)} %multiply_reduce_fusion.1), channel_id=1, source_target_pairs={{0,16},{16,0},{1,17},{17,1},{2,18},{18,2},{3,19},{19,3},{4,20},{20... | collective-permute-start | bytes 104 | tf_op jit(solution)/shard_map/ppermute | solution.py:85
  194.6 5.5 %collective-permute-start.10 = (f32[8]{0:T(128)S(1)}, f32[8]{0:T(128)S(1)}, u32[]{:S(2)}, u32[]{:S(2)}) collective-permute-start(f32[8]{0:T(128)S(1)} %add.434), channel_id=1, source_target_pairs={{0,1},{1,0},{2,3},{3,2},{4,5},{5,4},{6,7},{7,6},{8,9},{9,8},{10,11... | collective-permute-start | bytes 104 | tf_op jit(solution)/shard_map/ppermute | solution.py:85
  200.0 6.3 %collective-permute-start.11 = (f32[8]{0:T(128)S(1)}, f32[8]{0:T(128)S(1)}, u32[]{:S(2)}, u32[]{:S(2)}) collective-permute-start(f32[8]{0:T(128)S(1)} %add.435), channel_id=1, source_target_pairs={{0,2},{1,3},{2,0},{3,1},{4,6},{5,7},{6,4},{7,5},{8,10},{9,11},{10,... | collective-permute-start | bytes 104 | tf_op jit(solution)/shard_map/ppermute | solution.py:85
  206.4 9.4 %collective-permute-start.12 = (f32[8]{0:T(128)S(1)}, f32[8]{0:T(128)S(1)}, u32[]{:S(2)}, u32[]{:S(2)}) collective-permute-start(f32[8]{0:T(128)S(1)} %add.436), channel_id=1, source_target_pairs={{0,4},{1,5},{2,6},{3,7},{4,0},{5,1},{6,2},{7,3},{8,12},{9,13},{10,... | collective-permute-start | bytes 104 | tf_op jit(solution)/shard_map/ppermute | solution.py:85
  215.7 14.2 %collective-permute-start.13 = (f32[8]{0:T(128)S(1)}, f32[8]{0:T(128)S(1)}, u32[]{:S(2)}, u32[]{:S(2)}) collective-permute-start(f32[8]{0:T(128)S(1)} %add.437), channel_id=1, source_target_pairs={{0,8},{1,9},{2,10},{3,11},{4,12},{5,13},{6,14},{7,15},{8,0},{9,1},... | collective-permute-start | bytes 104 | tf_op jit(solution)/shard_map/ppermute | solution.py:85
Sparse Core Ops, SparseCore 0:
  11.3 64.3 all-gather.1
